TPU v7x, 512 devices: a whole 4x8x8 slice. The times are simulated.
512 devices in a mesh: seq: 64 (over z_hi, y, x), tp: 8 (over z_lo, core).
Axes of the slice: x: 4, y: 8, z: 8 (z_hi: 2, z_lo: 4; z = z_hi * 4 + z_lo), core: 2. Of those that a mesh axis runs over, the one named last changes fastest.
Arguments:
- residual: bfloat16 [16384, 5376], P('seq', 'tp'), may hold values from -10.5 to 10.5
- input_gain: float32 [5376], replicated, may hold values from 0.25 to 1.75
- w_query: bfloat16 [5376, 4096], P('seq', 'tp'), may hold values from -0.078125 to 0.078125
- key_weight: bfloat16 [5376, 2048], P('seq', 'tp'), may hold values from -0.078125 to 0.078125
- value_weight: bfloat16 [5376, 2048], P('seq', 'tp'), may hold values from -0.078125 to 0.078125
- query_gain: float32 [128], replicated, may hold values from 0.25 to 1.75
- key_gain: float32 [128], replicated, may hold values from 0.25 to 1.75
- w_out: bfloat16 [4096, 5376], P('tp', 'seq'), may hold values from -0.1640625 to 0.1640625
- post_gain: float32 [5376], replicated, may hold values from 0.25 to 1.75
- positions: int32 [16384], replicated, may hold values from 0 to 24063, as said below
Outputs:
- mixed: bfloat16 [16384, 5376], P('seq', 'tp')
Inputs may be any that keep to these rules, and one draw needn't show every extreme that they name: positions start at 0 and rise by 1 over the first 1024 tokens; after that they rise by 1 or 2 from each token to the next, by 2 at exactly (15360) // 2 tokens.
All inputs are finite; a program needn't handle non-finite values.
Results may differ from a plain program's by a relative error of at most 0.017.
Values may be sent and summed in bfloat16 or wider, within the bound.
No kernel may reach another device: no remote copies, remote signals or barrier semaphores. Data moves between devices by JAX's collectives and lax.ppermute only.
A program may use at most 128 MiB of HBM per device.

v0:
```python
import jax
import jax.numpy as jnp
from jax import lax
from jax.sharding import PartitionSpec as P

LOOKBACK_SPAN = 1024
epsilon = 1e-06
score_scale = 168.0 ** (-0.5)
rotary_base = 10000.0


def from_behind(block, axis, distance):
    devices = range(lax.axis_size(axis))
    route = [(i - distance, i) for i in devices if i - distance in devices]
    return lax.ppermute(block, axis, route)


def norm_scale(value_matrix, gain):
    mean_square = jnp.mean(value_matrix * value_matrix, axis=-1, keepdims=True)
    return value_matrix * lax.rsqrt(mean_square + epsilon) * gain


def rotary(value_matrix, places):
    half_dim = value_matrix.shape[-1] // 2
    inverse = rotary_base ** (-jnp.arange(half_dim, dtype=jnp.float32) / half_dim)
    angles = places.astype(jnp.float32)[:, None] * inverse[None, :]
    cosine = jnp.cos(angles)[:, None, :]
    sine = jnp.sin(angles)[:, None, :]
    first = value_matrix[..., :half_dim]
    second = value_matrix[..., half_dim:]
    return jnp.concatenate(
        [first * cosine - second * sine, second * cosine + first * sine], axis=-1
    )


def local(
    residual,
    input_gain,
    w_query,
    key_weight,
    value_weight,
    query_gain,
    key_gain,
    w_out,
    post_gain,
    positions,
):
    tok_rows = residual.shape[0]
    seq_at = lax.axis_index("seq")
    tp_at = lax.axis_index("tp")
    head_dim = query_gain.shape[0]
    local_kv = key_weight.shape[1] // head_dim
    query_group = w_query.shape[1] // key_weight.shape[1]
    gathered = lax.all_gather(residual, "tp", axis=1, tiled=True)
    normalized_input = norm_scale(gathered.astype(jnp.float32), input_gain).astype(jnp.bfloat16)
    own_places = lax.dynamic_slice_in_dim(positions, seq_at * tok_rows, tok_rows, 0)
    reach = (LOOKBACK_SPAN - 2) // tok_rows + 1

    def attend(query_matrix, stacked, key_places, valid):
        key_matrix = stacked[0].reshape(-1, local_kv, head_dim)
        value_matrix = stacked[1].reshape(-1, local_kv, head_dim)
        scores = (
            jnp.einsum(
                "qkgd,skd->kgqs", query_matrix, key_matrix, preferred_element_type=jnp.float32
            )
            * score_scale
        )
        distance = own_places[:, None] - key_places[None, :]
        allowed = valid[None, :] & (distance >= 0) & (distance < LOOKBACK_SPAN)
        weights = jnp.where(allowed[None, None], jnp.exp(scores), jnp.zeros_like(scores))
        total = jnp.sum(weights, axis=-1)
        summed = jnp.einsum(
            "kgqs,skd->qkgd",
            weights.astype(jnp.bfloat16),
            value_matrix,
            preferred_element_type=jnp.float32,
        )
        return (total, summed)

    pieces = (
        lax.all_gather(w_query, "seq", axis=0, tiled=True),
        lax.all_gather(key_weight, "seq", axis=0, tiled=True),
        lax.all_gather(value_weight, "seq", axis=0, tiled=True),
    )
    queries_raw, unrotated_keys, projected_values = tuple(
        (jnp.dot(normalized_input, piece, preferred_element_type=jnp.float32) for piece in pieces)
    )
    key_matrix = rotary(
        norm_scale(unrotated_keys.reshape(tok_rows, local_kv, head_dim), key_gain), own_places
    )
    stacked = jnp.stack(
        [key_matrix.reshape(tok_rows, local_kv * head_dim), projected_values]
    ).astype(jnp.bfloat16)
    pieces = []
    for distance in range(reach, 0, -1):
        pieces.append(from_behind(stacked, "seq", distance))
    halo = jnp.concatenate(pieces, axis=1)
    query_matrix = rotary(
        norm_scale(queries_raw.reshape(tok_rows, local_kv * query_group, head_dim), query_gain),
        own_places,
    )
    query_matrix = query_matrix.astype(jnp.bfloat16).reshape(
        tok_rows, local_kv, query_group, head_dim
    )
    inner_total, inner_sum = attend(
        query_matrix, stacked, own_places, jnp.ones((tok_rows,), jnp.bool_)
    )
    span = halo.shape[1]
    padded_places = jnp.concatenate([jnp.zeros((span,), jnp.int32), positions])
    halo_places = lax.dynamic_slice_in_dim(padded_places, seq_at * tok_rows, span, 0)
    halo_valid = seq_at * tok_rows - span + jnp.arange(span, dtype=jnp.int32) >= 0
    outer_total, outer_sum = attend(query_matrix, halo, halo_places, halo_valid)
    total = jnp.transpose(inner_total + outer_total, (2, 0, 1))
    merged = (inner_sum + outer_sum) / total[..., None]
    attended = merged.astype(jnp.bfloat16).reshape(tok_rows, local_kv * query_group * head_dim)
    partial_out = jnp.dot(
        attended,
        lax.all_gather(w_out, "seq", axis=1, tiled=True),
        preferred_element_type=jnp.float32,
    )
    summed_cols = lax.psum_scatter(
        partial_out.astype(jnp.bfloat16), "tp", scatter_dimension=1, tiled=True
    ).astype(jnp.float32)
    full_width = post_gain.shape[0]
    squares = lax.psum(jnp.sum(summed_cols * summed_cols, axis=1), "tp")
    inverse_rms = lax.rsqrt(squares / full_width + epsilon)
    gain_part = lax.dynamic_slice_in_dim(
        post_gain, tp_at * summed_cols.shape[1], summed_cols.shape[1], 0
    )
    return (residual.astype(jnp.float32) + summed_cols * inverse_rms[:, None] * gain_part).astype(
        jnp.bfloat16
    )


def solution(mesh):
    in_specs = (
        P("seq", "tp"),
        P(),
        P("seq", "tp"),
        P("seq", "tp"),
        P("seq", "tp"),
        P(),
        P(),
        P("tp", "seq"),
        P(),
        P(),
    )
    out_specs = P("seq", "tp")
    return jax.shard_map(local, mesh=mesh, in_specs=in_specs, out_specs=out_specs, check_vma=False)
```

profile of v0, /device:TPU:8, one launch (start us, length us, event | category | flops | bytes accessed | tf_op | source)
XLA Modules:
  0.0 810.8 jit_solution(6384950764701939511)
XLA Ops:
  12.1 46.5 %all-gather.10.cloned.1.call-done = bf16[256,5376]{0,1:T(8,128)(2,1)} async-done(((bf16[256,672]{0,1:T(8,128)(2,1)}), bf16[256,5376]{0,1:T(8,128)(2,1)}) %all-gather.10.cloned.1.call-update) | async-done | bytes 2752528 | tf_op jit(solution)/shard_map/all_gather | solution.py:54
  58.5 2.7 fusion
  61.2 146.3 %all-gather.14.cloned.1.call-done = bf16[64,84,256]{2,1,0:T(8,128)(2,1)} async-done(((bf16[1,84,256]{2,1,0:T(8,128)(2,1)}), bf16[64,84,256]{2,1,0:T(8,128)(2,1)}) %all-gather.14.cloned.1.call-update) | async-done | bytes 2752528 | tf_op jit(solution)/shard_map/all_gather | solution.py:82
  207.5 5.2 reshape.181
  212.7 3.5 multiply_reduce_fusion.1
  217.5 134.0 %all-gather.12.cloned.1.call-done = bf16[64,84,256]{2,1,0:T(8,128)(2,1)} async-done(((bf16[1,84,256]{2,1,0:T(8,128)(2,1)}), bf16[64,84,256]{2,1,0:T(8,128)(2,1)}) %all-gather.12.cloned.1.call-update) | async-done | bytes 2752528 | tf_op jit(solution)/shard_map/all_gather | solution.py:83
  351.5 5.2 reshape.179
  356.7 3.5 convolution_convert_fusion.1
  360.2 3.4 collective-permute-start
  364.4 4.7 collective-permute-start.1
  369.0 3.6 collective-permute-start.2
  373.5 2.9 collective-permute-start.3
  376.5 7.2 collective-permute-done.2
  383.7 4.6 collective-permute-done.3
  389.4 168.5 %all-gather.16.cloned.1.call-done = bf16[64,84,512]{2,1,0:T(8,128)(2,1)} async-done(((bf16[1,84,512]{2,1,0:T(8,128)(2,1)}), bf16[64,84,512]{2,1,0:T(8,128)(2,1)}) %all-gather.16.cloned.1.call-update) | async-done | bytes 5505040 | tf_op jit(solution)/shard_map/all_gather | solution.py:81
  557.9 8.9 %reshape.183 = bf16[5376,512]{1,0:T(8,128)(2,1)} reshape(bf16[64,84,512]{2,1,0:T(8,128)(2,1)} %all-gather.16.cloned.1.call-done) | data formatting | bytes 11010048
  566.8 6.5 fusion.40
  576.5 1.3 fusion.3
  579.0 151.3 %all-gather.18.cloned.1.call-done = bf16[64,84,512]{2,1,0:T(8,128)(2,1)} async-done(((bf16[1,84,512]{2,1,0:T(8,128)(2,1)}), bf16[64,84,512]{2,1,0:T(8,128)(2,1)}) %all-gather.18.cloned.1.call-update) | async-done | bytes 5505040 | tf_op jit(solution)/shard_map/all_gather | solution.py:118
  730.3 8.9 %reshape.185 = bf16[5376,512]{1,0:T(8,128)(2,1)} reshape(bf16[64,84,512]{2,1,0:T(8,128)(2,1)} %all-gather.18.cloned.1.call-done) | data formatting | bytes 11010048
  739.2 5.7 convolution_convert_fusion
  745.7 40.0 %reduce-scatter.2.cloned.1.call-done = bf16[256,672]{0,1:T(8,128)(2,1)} async-done(((bf16[256,5376]{0,1:T(8,128)(2,1)}), bf16[256,672]{0,1:T(8,128)(2,1)}) %reduce-scatter.2.cloned.1.call-update) | async-done | bytes 344080 | tf_op jit(solution)/shard_map/reduce_scatter | solution.py:121
  786.8 15.2 %psum.7 = f32[256]{0:T(256)S(1)} all-reduce(f32[256]{0:T(256)S(1)} %fusion.27), channel_id=1, replica_groups=mesh['seq'=64,'tp'=8] {'tp'}, use_global_device_ids=true, to_apply=%region_7.8 | all-reduce | flops 256 | bytes 2048 | tf_op jit(solution)/shard_map/psum | solution.py:125
  802.1 1.9 fusion.30
  (70 shorter events, 15.7 us)
Async XLA Ops:
  6.5 52.0 %all-gather.10.cloned.1.call-start = ((), (), s32[]{:S(2)}) async-start(), calls=%async_computation.1 | async-start | bytes 3096576 | tf_op jit(solution)/shard_map/all_gather | solution.py:54
  7.3 200.2 %all-gather.14.cloned.1.call-start = ((), (), s32[]{:S(2)}) async-start(), calls=%async_computation.4 | async-start | bytes 2928640 | tf_op jit(solution)/shard_map/all_gather | solution.py:82
  8.0 343.5 %all-gather.12.cloned.1.call-start = ((), (), s32[]{:S(2)}) async-start(), calls=%async_computation.3 | async-start | bytes 2928640 | tf_op jit(solution)/shard_map/all_gather | solution.py:83
  8.7 549.2 %all-gather.16.cloned.1.call-start = ((), (), s32[]{:S(2)}) async-start(), calls=%async_computation.5 | async-start | bytes 5857280 | tf_op jit(solution)/shard_map/all_gather | solution.py:81
  9.3 721.0 %all-gather.18.cloned.1.call-start = ((), (), s32[]{:S(2)}) async-start(), calls=%async_computation.6 | async-start | bytes 5857280 | tf_op jit(solution)/shard_map/all_gather | solution.py:118
  9.9 775.8 %reduce-scatter.2.cloned.1.call-start = ((), (), s32[]{:S(2)}) async-start(), calls=%async_computation.2 | async-start | bytes 3096576 | tf_op jit(solution)/shard_map/reduce_scatter | solution.py:121
  12.1 200.6 %copy-start.9 = (f32[5376]{0:T(1024)S(1)}, f32[5376]{0:T(1024)}, u32[]{:S(2)}) copy-start(f32[5376]{0:T(1024)} %param.11) | copy-start | bytes 64516
  58.5 154.1 %copy-start = (bf16[256,5376]{0,1:T(8,128)(2,1)S(1)}, bf16[256,5376]{0,1:T(8,128)(2,1)}, u32[]{:S(2)}) copy-start(bf16[256,5376]{0,1:T(8,128)(2,1)} %all-gather.10.cloned.1.call-done) | copy-start | bytes 8257540
  61.2 155.0 %copy-start.5 = (f32[256]{0:T(256)}, f32[256]{0:T(256)S(1)}, u32[]{:S(2)}) copy-start(f32[256]{0:T(256)S(1)} %add_rsqrt_fusion.3) | copy-start | bytes 3076
  216.3 140.4 %copy-start.6 = (f32[256]{0:T(256)S(1)}, f32[256]{0:T(256)}, u32[]{:S(2)}) copy-start(f32[256]{0:T(256)} %copy-done.5) | copy-start | bytes 3076
  216.3 140.3 %copy-start.10 = (f32[5376]{0:T(1024)S(1)}, f32[5376]{0:T(1024)}, u32[]{:S(2)}) copy-start(f32[5376]{0:T(1024)} %param.11) | copy-start | bytes 64516
  360.2 16.2 %collective-permute-start = (bf16[2,256,256]{1,2,0:T(8,128)(2,1)S(1)}, bf16[2,256,256]{1,2,0:T(8,128)(2,1)S(1)}, u32[]{:S(2)}, u32[]{:S(2)}) collective-permute-start(bf16[2,256,256]{1,2,0:T(8,128)(2,1)S(1)} %pad_maximum_fusion.1), channel_id=1, source_target_pairs={{0,32},{8,40},{16,48},{24,56},{32,64},{40,72},{48,80},{56,88},{64,... | collective-permute-start | bytes 786440 | tf_op jit(solution)/shard_map/ppermute | solution.py:15
  364.4 12.1 %collective-permute-start.1 = (bf16[2,256,256]{1,2,0:T(8,128)(2,1)S(1)}, bf16[2,256,256]{1,2,0:T(8,128)(2,1)S(1)}, u32[]{:S(2)}, u32[]{:S(2)}) collective-permute-start(bf16[2,256,256]{1,2,0:T(8,128)(2,1)S(1)} %pad_maximum_fusion.1), channel_id=1, source_target_pairs={{0,24},{8,32},{16,40},{24,48},{32,56},{40,64},{48,72},{56,80},{64,... | collective-permute-start | bytes 786440 | tf_op jit(solution)/shard_map/ppermute | solution.py:15
  369.0 14.6 %collective-permute-start.2 = (bf16[2,256,256]{1,2,0:T(8,128)(2,1)S(1)}, bf16[2,256,256]{1,2,0:T(8,128)(2,1)S(1)}, u32[]{:S(2)}, u32[]{:S(2)}) collective-permute-start(bf16[2,256,256]{1,2,0:T(8,128)(2,1)S(1)} %pad_maximum_fusion.1), channel_id=1, source_target_pairs={{0,16},{8,24},{16,32},{24,40},{32,48},{40,56},{48,64},{56,72},{64,... | collective-permute-start | bytes 786440 | tf_op jit(solution)/shard_map/ppermute | solution.py:15
  373.5 14.8 %collective-permute-start.3 = (bf16[2,256,256]{1,2,0:T(8,128)(2,1)S(1)}, bf16[2,256,256]{1,2,0:T(8,128)(2,1)S(1)}, u32[]{:S(2)}, u32[]{:S(2)}) collective-permute-start(bf16[2,256,256]{1,2,0:T(8,128)(2,1)S(1)} %pad_maximum_fusion.1), channel_id=1, source_target_pairs={{0,8},{8,16},{16,24},{24,32},{32,40},{40,48},{48,56},{56,64},{64,7... | collective-permute-start | bytes 786440 | tf_op jit(solution)/shard_map/ppermute | solution.py:15
  389.4 177.4 %copy-start.7 = (f32[256]{0:T(256)S(1)}, f32[256]{0:T(256)}, u32[]{:S(2)}) copy-start(f32[256]{0:T(256)} %copy-done.5) | copy-start | bytes 3076
  566.8 8.2 %copy-start.8 = (f32[128]{0:T(128)S(1)}, f32[128]{0:T(128)}, u32[]{:S(2)}) copy-start(f32[128]{0:T(128)} %param.15) | copy-start | bytes 1540
  573.3 2.6 copy-start.4
  573.3 3.1 copy-start.3
  576.5 1.6 copy-start.2
  739.2 62.9 %copy-start.1 = (bf16[256,672]{0,1:T(8,128)(2,1)S(1)}, bf16[256,672]{0,1:T(8,128)(2,1)}, u32[]{:S(2)}) copy-start(bf16[256,672]{0,1:T(8,128)(2,1)} %param.10) | copy-start | bytes 1032196
Sparse Core Ops, SparseCore 0:
  9.4 49.0 all-gather.9
  63.1 144.3 all-gather.13
  212.1 139.3 all-gather.11
  355.9 201.9 all-gather.15
  562.2 167.9 all-gather.17
  745.0 40.6 reduce-scatter.1
where the time goes:
time: 812 us; the launch traced here: 811 us
  waiting for transfers between devices  701 us (86%)
  local copies, waits for them, and re-layouts  32.4 us (4%)
  matrix products  22.3 us (3%)
  blocking collectives  15.2 us (2%)
  starting transfers between devices  14.8 us (2%)
  between operations  13.8 us (2%)
  other arithmetic  10.9 us (1%)
    all_gather x1, waiting for transfers between devices, local(): lax.all_gather(w_query, 'seq', axis=0, tiled=True)  169 us
    all_gather x1, waiting for transfers between devices, local(): lax.all_gather(w_out, 'seq', axis=1, tiled=True)  151 us
    all_gather x1, waiting for transfers between devices, local(): lax.all_gather(key_weight, 'seq', axis=0, tiled=True)  146 us
    all_gather x1, waiting for transfers between devices, local(): lax.all_gather(value_weight, 'seq', axis=0, tiled=True)  134 us
    all_gather x1, waiting for transfers between devices, local(): gathered = lax.all_gather(residual, 'tp', axis=1, tiled=True)  46.5 us
    reduce_scatter x1, waiting for transfers between devices, local(): lax.psum_scatter(partial_out.astype(jnp.bfloat16), 'tp', scatter_dimensio...  40 us
    unnamed x29, local copies, waits for them, and re-layouts  28.2 us
  transfers between devices with their start and end apart: 10, of which 8 were waited for; matrix products, arithmetic and copies ran while one was open for 6% of the time, Pallas kernels for 0%

commit v1 on v0

--- a/solution.py
+++ b/solution.py
@@ -80,7 +80,9 @@
     pieces = (
         lax.all_gather(w_query, "seq", axis=0, tiled=True),
         lax.all_gather(key_weight, "seq", axis=0, tiled=True),
-        lax.all_gather(value_weight, "seq", axis=0, tiled=True),
+        jnp.concatenate(
+            lax.all_to_all(jnp.stack([value_weight] * lax.axis_size("seq")), "seq", 0, 0), axis=0
+        ),
     )
     queries_raw, unrotated_keys, projected_values = tuple(
         (jnp.dot(normalized_input, piece, preferred_element_type=jnp.float32) for piece in pieces)

time: 812 us -> 702 us (0.86)
  the two profiles are of different devices: /device:TPU:8 before, /device:TPU:2 now
where the time goes in v1:
time: 702 us; the launch traced here: 700 us
  waiting for transfers between devices  572 us (81%)
  starting transfers between devices  33.3 us (5%)
  local copies, waits for them, and re-layouts  32.3 us (5%)
  matrix products  24.7 us (4%)
  blocking collectives  15.1 us (2%)
  between operations  13.5 us (2%)
  other arithmetic  9.41 us (1%)
    all_gather x1, waiting for transfers between devices, local(): lax.all_gather(w_out, 'seq', axis=1, tiled=True)  151 us
    all_gather x1, waiting for transfers between devices, local(): lax.all_gather(key_weight, 'seq', axis=0, tiled=True)  147 us
    all_gather x1, waiting for transfers between devices, local(): lax.all_gather(w_query, 'seq', axis=0, tiled=True)  138 us
    all_gather x1, waiting for transfers between devices, local(): gathered = lax.all_gather(residual, 'tp', axis=1, tiled=True)  89 us
    reduce_scatter x1, waiting for transfers between devices, local(): lax.psum_scatter(partial_out.astype(jnp.bfloat16), 'tp', scatter_dimensio...  39.8 us
    unnamed x24, local copies, waits for them, and re-layouts  23 us
    all_to_all x1, starting transfers between devices, local(): lax.all_to_all(jnp.stack([value_weight] * lax.axis_size('seq')), 'seq', 0...  19.1 us
    dot_general x3, matrix products, local(): jnp.dot(normalized_input, piece, preferred_element_type=jnp.float32)  15.9 us
  transfers between devices with their start and end apart: 10, of which 6 were waited for; matrix products, arithmetic and copies ran while one was open for 7% of the time, Pallas kernels for 0%

profile of v1, /device:TPU:2, one launch (start us, length us, event | category | flops | bytes accessed | tf_op | source)
XLA Modules:
  0.0 700.5 jit_solution(4153090253099060304)
XLA Ops:
  9.3 2.5 stack.8
  11.9 19.1 %all-to-all-start = ((bf16[64,84,256]{2,1,0:T(8,128)(2,1)}), bf16[64,84,256]{2,1,0:T(8,128)(2,1)S(1)}, u32[]{:S(2)}, u32[]{:S(2)}) async-start(bf16[64,84,256]{2,1,0:T(8,128)(2,1)} %stack.8), calls=%async_computation | async-start | bytes 5767168 | tf_op jit(solution)/shard_map/all_to_all | solution.py:84
  31.8 89.0 %all-gather.8.cloned.1.call-done = bf16[256,5376]{0,1:T(8,128)(2,1)} async-done(((bf16[256,672]{0,1:T(8,128)(2,1)}), bf16[256,5376]{0,1:T(8,128)(2,1)}) %all-gather.8.cloned.1.call-update) | async-done | bytes 2752528 | tf_op jit(solution)/shard_map/all_gather | solution.py:54
  120.8 2.5 fusion
  123.3 147.3 %all-gather.10.cloned.1.call-done = bf16[64,84,256]{2,1,0:T(8,128)(2,1)} async-done(((bf16[1,84,256]{2,1,0:T(8,128)(2,1)}), bf16[64,84,256]{2,1,0:T(8,128)(2,1)}) %all-gather.10.cloned.1.call-update) | async-done | bytes 2752528 | tf_op jit(solution)/shard_map/all_gather | solution.py:82
  270.6 5.2 reshape.185
  275.8 5.0 multiply_reduce_fusion.1
  282.5 2.3 reshape.180
  284.7 4.3 convolution_convert_fusion.1
  289.1 2.6 collective-permute-start
  292.5 3.3 collective-permute-start.1
  295.8 4.3 collective-permute-start.2
  300.8 3.9 collective-permute-start.3
  304.8 4.3 collective-permute-done.3
  310.3 137.9 %all-gather.12.cloned.1.call-done = bf16[64,84,512]{2,1,0:T(8,128)(2,1)} async-done(((bf16[1,84,512]{2,1,0:T(8,128)(2,1)}), bf16[64,84,512]{2,1,0:T(8,128)(2,1)}) %all-gather.12.cloned.1.call-update) | async-done | bytes 5505040 | tf_op jit(solution)/shard_map/all_gather | solution.py:81
  448.2 8.9 %reshape.187 = bf16[5376,512]{1,0:T(8,128)(2,1)} reshape(bf16[64,84,512]{2,1,0:T(8,128)(2,1)} %all-gather.12.cloned.1.call-done) | data formatting | bytes 11010048
  457.1 6.6 fusion.40
  466.8 1.3 fusion.3
  469.3 151.2 %all-gather.14.cloned.1.call-done = bf16[64,84,512]{2,1,0:T(8,128)(2,1)} async-done(((bf16[1,84,512]{2,1,0:T(8,128)(2,1)}), bf16[64,84,512]{2,1,0:T(8,128)(2,1)}) %all-gather.14.cloned.1.call-update) | async-done | bytes 5505040 | tf_op jit(solution)/shard_map/all_gather | solution.py:120
  620.6 8.9 %reshape.189 = bf16[5376,512]{1,0:T(8,128)(2,1)} reshape(bf16[64,84,512]{2,1,0:T(8,128)(2,1)} %all-gather.14.cloned.1.call-done) | data formatting | bytes 11010048
  629.5 5.7 convolution_convert_fusion
  636.0 39.8 %reduce-scatter.2.cloned.1.call-done = bf16[256,672]{0,1:T(8,128)(2,1)} async-done(((bf16[256,5376]{0,1:T(8,128)(2,1)}), bf16[256,672]{0,1:T(8,128)(2,1)}) %reduce-scatter.2.cloned.1.call-update) | async-done | bytes 344080 | tf_op jit(solution)/shard_map/reduce_scatter | solution.py:123
  676.9 15.1 %psum.7 = f32[256]{0:T(256)S(1)} all-reduce(f32[256]{0:T(256)S(1)} %fusion.27), channel_id=1, replica_groups=mesh['seq'=64,'tp'=8] {'tp'}, use_global_device_ids=true, to_apply=%region_7.8 | all-reduce | flops 256 | bytes 2048 | tf_op jit(solution)/shard_map/psum | solution.py:127
  692.0 1.9 fusion.30
  (66 shorter events, 14.0 us)
Async XLA Ops:
  6.5 114.2 %all-gather.8.cloned.1.call-start = ((), (), s32[]{:S(2)}) async-start(), calls=%async_computation.2 | async-start | bytes 3096576 | tf_op jit(solution)/shard_map/all_gather | solution.py:54
  7.3 263.3 %all-gather.10.cloned.1.call-start = ((), (), s32[]{:S(2)}) async-start(), calls=%async_computation.4 | async-start | bytes 2928640 | tf_op jit(solution)/shard_map/all_gather | solution.py:82
  8.0 440.2 %all-gather.12.cloned.1.call-start = ((), (), s32[]{:S(2)}) async-start(), calls=%async_computation.5 | async-start | bytes 5857280 | tf_op jit(solution)/shard_map/all_gather | solution.py:81
  8.7 611.8 %all-gather.14.cloned.1.call-start = ((), (), s32[]{:S(2)}) async-start(), calls=%async_computation.6 | async-start | bytes 5857280 | tf_op jit(solution)/shard_map/all_gather | solution.py:120
  9.3 21.7 %copy-start.4 = (s32[16384]{0:T(1024)S(1)}, s32[16384]{0:T(1024)}, u32[]{:S(2)}) copy-start(s32[16384]{0:T(1024)} %param.19) | copy-start | bytes 196612
  11.9 270.6 %all-to-all-start = ((bf16[64,84,256]{2,1,0:T(8,128)(2,1)}), bf16[64,84,256]{2,1,0:T(8,128)(2,1)S(1)}, u32[]{:S(2)}, u32[]{:S(2)}) async-start(bf16[64,84,256]{2,1,0:T(8,128)(2,1)} %stack.8), calls=%async_computation | async-start | bytes 5767168 | tf_op jit(solution)/shard_map/all_to_all | solution.py:84
  31.0 644.8 %reduce-scatter.2.cloned.1.call-start = ((), (), s32[]{:S(2)}) async-start(), calls=%async_computation.3 | async-start | bytes 3096576 | tf_op jit(solution)/shard_map/reduce_scatter | solution.py:123
  31.8 244.0 %copy-start.8 = (f32[5376]{0:T(1024)S(1)}, f32[5376]{0:T(1024)}, u32[]{:S(2)}) copy-start(f32[5376]{0:T(1024)} %param.11) | copy-start | bytes 64516
  275.8 6.1 copy-start.6
  289.1 15.6 %collective-permute-start = (bf16[2,256,256]{1,2,0:T(8,128)(2,1)S(1)}, bf16[2,256,256]{1,2,0:T(8,128)(2,1)S(1)}, u32[]{:S(2)}, u32[]{:S(2)}) collective-permute-start(bf16[2,256,256]{1,2,0:T(8,128)(2,1)S(1)} %pad_maximum_fusion.1), channel_id=1, source_target_pairs={{0,32},{8,40},{16,48},{24,56},{32,64},{40,72},{48,80},{56,88},{64,... | collective-permute-start | bytes 786440 | tf_op jit(solution)/shard_map/ppermute | solution.py:15
  292.5 12.3 %collective-permute-start.1 = (bf16[2,256,256]{1,2,0:T(8,128)(2,1)S(1)}, bf16[2,256,256]{1,2,0:T(8,128)(2,1)S(1)}, u32[]{:S(2)}, u32[]{:S(2)}) collective-permute-start(bf16[2,256,256]{1,2,0:T(8,128)(2,1)S(1)} %pad_maximum_fusion.1), channel_id=1, source_target_pairs={{0,24},{8,32},{16,40},{24,48},{32,56},{40,64},{48,72},{56,80},{64,... | collective-permute-start | bytes 786440 | tf_op jit(solution)/shard_map/ppermute | solution.py:15
  295.8 9.0 %collective-permute-start.2 = (bf16[2,256,256]{1,2,0:T(8,128)(2,1)S(1)}, bf16[2,256,256]{1,2,0:T(8,128)(2,1)S(1)}, u32[]{:S(2)}, u32[]{:S(2)}) collective-permute-start(bf16[2,256,256]{1,2,0:T(8,128)(2,1)S(1)} %pad_maximum_fusion.1), channel_id=1, source_target_pairs={{0,16},{8,24},{16,32},{24,40},{32,48},{40,56},{48,64},{56,72},{64,... | collective-permute-start | bytes 786440 | tf_op jit(solution)/shard_map/ppermute | solution.py:15
  300.8 8.3 %collective-permute-start.3 = (bf16[2,256,256]{1,2,0:T(8,128)(2,1)S(1)}, bf16[2,256,256]{1,2,0:T(8,128)(2,1)S(1)}, u32[]{:S(2)}, u32[]{:S(2)}) collective-permute-start(bf16[2,256,256]{1,2,0:T(8,128)(2,1)S(1)} %pad_maximum_fusion.1), channel_id=1, source_target_pairs={{0,8},{8,16},{16,24},{24,32},{32,40},{40,48},{48,56},{56,64},{64,7... | collective-permute-start | bytes 786440 | tf_op jit(solution)/shard_map/ppermute | solution.py:15
  310.3 146.8 %copy-start = (bf16[256,5376]{0,1:T(8,128)(2,1)S(1)}, bf16[256,5376]{0,1:T(8,128)(2,1)}, u32[]{:S(2)}) copy-start(bf16[256,5376]{0,1:T(8,128)(2,1)} %all-gather.8.cloned.1.call-done) | copy-start | bytes 8257540
  457.1 8.2 %copy-start.7 = (f32[128]{0:T(128)S(1)}, f32[128]{0:T(128)}, u32[]{:S(2)}) copy-start(f32[128]{0:T(128)} %param.15) | copy-start | bytes 1540
  463.6 2.6 copy-start.5
  463.6 3.1 copy-start.3
  466.7 1.6 copy-start.2
  629.5 62.6 %copy-start.1 = (bf16[256,672]{0,1:T(8,128)(2,1)S(1)}, bf16[256,672]{0,1:T(8,128)(2,1)}, u32[]{:S(2)}) copy-start(bf16[256,672]{0,1:T(8,128)(2,1)} %param.10) | copy-start | bytes 1032196
Sparse Core Ops, SparseCore 0:
  9.4 111.2 all-gather.7
  125.3 145.2 all-gather.9
  275.1 173.0 all-gather.11
  452.5 167.9 all-gather.13
  635.3 40.3 reduce-scatter.1
